TPU v7x, 32 devices: a whole 2x2x4 slice. The times are simulated.
32 devices in a mesh: ctx: 8 (over z, y), tp: 4 (over x, core).
Axes of the slice: x: 2, y: 2, z: 4, core: 2. Of those that a mesh axis runs over, the one named last changes fastest.
Arguments:
- queries: bfloat16 [2048, 16, 128], P('ctx', 'tp'), may hold values from -12 to 12
- keys: bfloat16 [2048, 8, 128], P('ctx', 'tp'), may hold values from -6 to 6
- values: bfloat16 [2048, 8, 128], P('ctx', 'tp'), may hold values from -6 to 6
- residual: bfloat16 [2048, 3072], P('ctx', 'tp'), may hold values from -6 to 6
- out_weight: bfloat16 [16, 128, 3072], P(None, None, 'tp'), may hold values from -1 to 1
- post_gain: bfloat16 [3072], P('tp'), may hold values from 0.099609375 to 1.8984375
Outputs:
- mixed: bfloat16 [2048, 3072], P('ctx', 'tp')
All inputs are finite; a program needn't handle non-finite values.
Results may differ from a plain program's by a relative error of at most 0.015.
Values may be sent and summed in bfloat16 or wider, within the bound.
No kernel may reach another device: no remote copies, remote signals or barrier semaphores. Data moves between devices by JAX's collectives and lax.ppermute only.
A program may use at most 64 MiB of HBM per device.

v0:
```python
import jax
import jax.numpy as jnp
from jax import lax
from jax.sharding import PartitionSpec as P

WINDOW_TOKENS = 4096
D = 3072
softcap_value = 50.0
query_scale = 1.0 / 12.0
rope_base = 10000.0


def passed_along(value, axis, steps):
    count = lax.axis_size(axis)
    first, last = (max(0, -steps), min(count, count - steps))
    return lax.ppermute(value, axis, [(source, source + steps) for source in range(first, last)])


def rotate(values_in, positions):
    half_width = values_in.shape[-1] // 2
    steps_half = jnp.arange(half_width, dtype=jnp.float32)
    inverse = rope_base ** (-2.0 * steps_half / values_in.shape[-1])
    angles = positions.astype(jnp.float32)[..., None] * inverse
    cosine = jnp.cos(angles)
    sine_part = jnp.sin(angles)
    first_half = values_in[..., :half_width]
    second_half = values_in[..., half_width:]
    return jnp.concatenate(
        [
            first_half * cosine - second_half * sine_part,
            second_half * cosine + first_half * sine_part,
        ],
        axis=-1,
    )


def attend_block(state, key_block, value_block, source, rotary_queries, device_index):
    numerators, denominators = state
    rows = key_block.shape[0]
    scores = (
        jnp.einsum("sgrh,kgh->grsk", rotary_queries, key_block, preferred_element_type=jnp.float32)
        * query_scale
    )
    capped = softcap_value * jnp.tanh(scores / softcap_value)
    offsets = jnp.arange(rows, dtype=jnp.int32)
    query_pos = device_index * rows + offsets
    key_pos = source * rows + offsets
    distance = query_pos[:, None] - key_pos[None, :]
    allowed = (distance >= 0) & (distance < WINDOW_TOKENS) & (key_pos[None, :] >= 0)
    weights = jnp.where(allowed[None, None], jnp.exp(capped), 0.0)
    denominators = denominators + jnp.sum(weights, axis=-1)
    numerators = numerators + jnp.einsum(
        "grsk,kgh->grsh",
        weights.astype(jnp.bfloat16),
        value_block,
        preferred_element_type=jnp.float32,
    )
    return (numerators, denominators)


def local(queries, keys, values, residual, out_weight, post_gain):
    rows = queries.shape[0]
    q_heads = queries.shape[1]
    head_size = queries.shape[2]
    kv_heads = keys.shape[1]
    heads_per_group = q_heads // kv_heads
    cycle_size = lax.axis_size("ctx")
    device_index = lax.axis_index("ctx")
    positions = (device_index * rows + jnp.arange(rows, dtype=jnp.int32))[:, None]
    rotary_queries = rotate(queries.astype(jnp.float32), positions).astype(jnp.bfloat16)
    rotary_queries = rotary_queries.reshape(rows, kv_heads, heads_per_group, head_size)
    rotary_keys = rotate(keys.astype(jnp.float32), positions).astype(jnp.bfloat16)
    reach = min(WINDOW_TOKENS // rows, cycle_size - 1)
    state = (
        jnp.zeros((kv_heads, heads_per_group, rows, head_size), jnp.float32),
        jnp.zeros((kv_heads, heads_per_group, rows), jnp.float32),
    )
    state = attend_block(state, rotary_keys, values, device_index, rotary_queries, device_index)

    def advance(step_index, carried):
        running, key_block, value_block = carried
        key_block, value_block = passed_along((key_block, value_block), "ctx", 1)
        running = attend_block(
            running,
            key_block,
            value_block,
            device_index - step_index - 1,
            rotary_queries,
            device_index,
        )
        return (running, key_block, value_block)

    state, unused_keys, unused_values = lax.fori_loop(
        0, reach, advance, (state, rotary_keys, values)
    )
    numerators, denominators = state
    attended = (numerators / denominators[..., None]).astype(jnp.bfloat16)
    attended = jnp.transpose(attended, (2, 0, 1, 3)).reshape(rows, q_heads, head_size)
    local_cols = out_weight.shape[2]
    piece = lax.all_gather(attended, "tp", axis=1, tiled=True)
    heads_in = piece.shape[1]
    weight_rows = out_weight.reshape(heads_in * head_size, local_cols)
    projected = jnp.dot(
        piece.reshape(rows, heads_in * head_size), weight_rows, preferred_element_type=jnp.float32
    )
    square_sums = lax.psum(jnp.sum(projected * projected, axis=1), "tp")
    normed = projected * lax.rsqrt(square_sums / D + 1e-06)[:, None] * post_gain.astype(jnp.float32)
    mixed = residual.astype(jnp.float32) + normed
    return mixed.astype(jnp.bfloat16)


def solution(mesh):
    in_specs = (
        P("ctx", "tp", None),
        P("ctx", "tp", None),
        P("ctx", "tp", None),
        P("ctx", "tp"),
        P(None, None, "tp"),
        P("tp"),
    )
    out_specs = P("ctx", "tp")
    return jax.shard_map(local, mesh=mesh, in_specs=in_specs, out_specs=out_specs, check_vma=False)
```

profile of v0, /device:TPU:0, one launch (start us, length us, event | category | flops | bytes accessed | tf_op | source)
XLA Modules:
  0.0 137.2 jit_solution(11933492602181658960)
XLA Ops:
  16.1 85.1 %while.21 = (s32[]{:T(128)}, f32[2,2,256,128]{3,2,1,0:T(8,128)}, f32[2,2,256]{2,1,0:T(2,128)S(1)}, bf16[256,2,128]{2,0,1:T(8,128)(2,1)}, bf16[256,2,128]{2,0,1:T...) while((s32[]{:T(128)}, f32[2,2,256,128]{3,2,1,0:T(8,128)}, ...), condition=%wide.region_3.4_spmd, body=%wide.region_1.3_spmd.sunk | while | flops 135988224 | bytes 8540965 | solution.py:93
  16.1 4.9 %collective-permute-start = (bf16[256,2,128]{2,0,1:T(8,128)(2,1)}, bf16[256,2,128]{2,0,1:T(8,128)(2,1)S(1)}, u32[]{:S(2)}, u32[]{:S(2)}) collective-permute-start(bf16[256,2,128]{2,0,1:T(8,128)(2,1)} %get-tuple-element.308), channel_id=1, source_target_pairs={{0,4},{4,8},{8,12},{12,16},{16,20},{20,24},{24,28},{1,5},{5,9},{9,... | collective-permute-start | bytes 393224 | tf_op jit(solution)/shard_map/while/body/eval_jaxpr/ppermute | solution.py:16
  21.0 3.4 %collective-permute-start.1 = (bf16[256,2,128]{2,0,1:T(8,128)(2,1)S(1)}, bf16[256,2,128]{2,0,1:T(8,128)(2,1)S(1)}, u32[]{:S(2)}, u32[]{:S(2)}) collective-permute-start(bf16[256,2,128]{2,0,1:T(8,128)(2,1)S(1)} %get-tuple-element.309), channel_id=1, source_target_pairs={{0,4},{4,8},{8,12},{12,16},{16,20},{20,24},{24,28},{1,5},{5,9},{9,... | collective-permute-start | bytes 393224 | tf_op jit(solution)/shard_map/while/body/eval_jaxpr/ppermute | solution.py:16
  24.7 1.4 %fusion.40 = (f32[2,2,256]{2,1,0:T(2,128)S(1)}, bf16[2,2,256,256]{2,3,1,0:T(8,128)(2,1)S(1)}) fusion(bf16[256,2,2,128]{3,0,2,1:T(8,128)(2,1)} %get-tuple-element.323, bf16[256,2,128]{2,0,1:T(8,128)(2,1)S(1)} %collective-permute-done, pred[256,256]{0,1:T(8,128)(4,1)S(1)} %fusion.39), kind=kOutput, calls=%fused_computation.49.clone.1 | convolution fusion | flops 68418560 | bytes 987136 | tf_op jit(solution)/shard_map/while/body/eval_jaxpr/sgrh,kgh->grsk/dot_general | solution.py:41
  28.2 4.3 %collective-permute-start = (bf16[256,2,128]{2,0,1:T(8,128)(2,1)}, bf16[256,2,128]{2,0,1:T(8,128)(2,1)S(1)}, u32[]{:S(2)}, u32[]{:S(2)}) collective-permute-start(bf16[256,2,128]{2,0,1:T(8,128)(2,1)} %get-tuple-element.308), channel_id=1, source_target_pairs={{0,4},{4,8},{8,12},{12,16},{16,20},{20,24},{24,28},{1,5},{5,9},{9,... | collective-permute-start | bytes 393224 | tf_op jit(solution)/shard_map/while/body/eval_jaxpr/ppermute | solution.py:16
  32.5 4.3 %collective-permute-start.1 = (bf16[256,2,128]{2,0,1:T(8,128)(2,1)S(1)}, bf16[256,2,128]{2,0,1:T(8,128)(2,1)S(1)}, u32[]{:S(2)}, u32[]{:S(2)}) collective-permute-start(bf16[256,2,128]{2,0,1:T(8,128)(2,1)S(1)} %get-tuple-element.309), channel_id=1, source_target_pairs={{0,4},{4,8},{8,12},{12,16},{16,20},{20,24},{24,28},{1,5},{5,9},{9,... | collective-permute-start | bytes 393224 | tf_op jit(solution)/shard_map/while/body/eval_jaxpr/ppermute | solution.py:16
  40.6 4.3 %collective-permute-start = (bf16[256,2,128]{2,0,1:T(8,128)(2,1)}, bf16[256,2,128]{2,0,1:T(8,128)(2,1)S(1)}, u32[]{:S(2)}, u32[]{:S(2)}) collective-permute-start(bf16[256,2,128]{2,0,1:T(8,128)(2,1)} %get-tuple-element.308), channel_id=1, source_target_pairs={{0,4},{4,8},{8,12},{12,16},{16,20},{20,24},{24,28},{1,5},{5,9},{9,... | collective-permute-start | bytes 393224 | tf_op jit(solution)/shard_map/while/body/eval_jaxpr/ppermute | solution.py:16
  45.0 4.1 %collective-permute-start.1 = (bf16[256,2,128]{2,0,1:T(8,128)(2,1)S(1)}, bf16[256,2,128]{2,0,1:T(8,128)(2,1)S(1)}, u32[]{:S(2)}, u32[]{:S(2)}) collective-permute-start(bf16[256,2,128]{2,0,1:T(8,128)(2,1)S(1)} %get-tuple-element.309), channel_id=1, source_target_pairs={{0,4},{4,8},{8,12},{12,16},{16,20},{20,24},{24,28},{1,5},{5,9},{9,... | collective-permute-start | bytes 393224 | tf_op jit(solution)/shard_map/while/body/eval_jaxpr/ppermute | solution.py:16
  52.8 4.4 %collective-permute-start = (bf16[256,2,128]{2,0,1:T(8,128)(2,1)}, bf16[256,2,128]{2,0,1:T(8,128)(2,1)S(1)}, u32[]{:S(2)}, u32[]{:S(2)}) collective-permute-start(bf16[256,2,128]{2,0,1:T(8,128)(2,1)} %get-tuple-element.308), channel_id=1, source_target_pairs={{0,4},{4,8},{8,12},{12,16},{16,20},{20,24},{24,28},{1,5},{5,9},{9,... | collective-permute-start | bytes 393224 | tf_op jit(solution)/shard_map/while/body/eval_jaxpr/ppermute | solution.py:16
  57.2 3.7 %collective-permute-start.1 = (bf16[256,2,128]{2,0,1:T(8,128)(2,1)S(1)}, bf16[256,2,128]{2,0,1:T(8,128)(2,1)S(1)}, u32[]{:S(2)}, u32[]{:S(2)}) collective-permute-start(bf16[256,2,128]{2,0,1:T(8,128)(2,1)S(1)} %get-tuple-element.309), channel_id=1, source_target_pairs={{0,4},{4,8},{8,12},{12,16},{16,20},{20,24},{24,28},{1,5},{5,9},{9,... | collective-permute-start | bytes 393224 | tf_op jit(solution)/shard_map/while/body/eval_jaxpr/ppermute | solution.py:16
  61.1 1.4 %fusion.40 = (f32[2,2,256]{2,1,0:T(2,128)S(1)}, bf16[2,2,256,256]{2,3,1,0:T(8,128)(2,1)S(1)}) fusion(bf16[256,2,2,128]{3,0,2,1:T(8,128)(2,1)} %get-tuple-element.323, bf16[256,2,128]{2,0,1:T(8,128)(2,1)S(1)} %collective-permute-done, pred[256,256]{0,1:T(8,128)(4,1)S(1)} %fusion.39), kind=kOutput, calls=%fused_computation.49.clone.1 | convolution fusion | flops 68418560 | bytes 987136 | tf_op jit(solution)/shard_map/while/body/eval_jaxpr/sgrh,kgh->grsk/dot_general | solution.py:41
  64.6 4.3 %collective-permute-start = (bf16[256,2,128]{2,0,1:T(8,128)(2,1)}, bf16[256,2,128]{2,0,1:T(8,128)(2,1)S(1)}, u32[]{:S(2)}, u32[]{:S(2)}) collective-permute-start(bf16[256,2,128]{2,0,1:T(8,128)(2,1)} %get-tuple-element.308), channel_id=1, source_target_pairs={{0,4},{4,8},{8,12},{12,16},{16,20},{20,24},{24,28},{1,5},{5,9},{9,... | collective-permute-start | bytes 393224 | tf_op jit(solution)/shard_map/while/body/eval_jaxpr/ppermute | solution.py:16
  69.0 4.1 %collective-permute-start.1 = (bf16[256,2,128]{2,0,1:T(8,128)(2,1)S(1)}, bf16[256,2,128]{2,0,1:T(8,128)(2,1)S(1)}, u32[]{:S(2)}, u32[]{:S(2)}) collective-permute-start(bf16[256,2,128]{2,0,1:T(8,128)(2,1)S(1)} %get-tuple-element.309), channel_id=1, source_target_pairs={{0,4},{4,8},{8,12},{12,16},{16,20},{20,24},{24,28},{1,5},{5,9},{9,... | collective-permute-start | bytes 393224 | tf_op jit(solution)/shard_map/while/body/eval_jaxpr/ppermute | solution.py:16
  76.8 4.3 %collective-permute-start = (bf16[256,2,128]{2,0,1:T(8,128)(2,1)}, bf16[256,2,128]{2,0,1:T(8,128)(2,1)S(1)}, u32[]{:S(2)}, u32[]{:S(2)}) collective-permute-start(bf16[256,2,128]{2,0,1:T(8,128)(2,1)} %get-tuple-element.308), channel_id=1, source_target_pairs={{0,4},{4,8},{8,12},{12,16},{16,20},{20,24},{24,28},{1,5},{5,9},{9,... | collective-permute-start | bytes 393224 | tf_op jit(solution)/shard_map/while/body/eval_jaxpr/ppermute | solution.py:16
  81.1 3.7 %collective-permute-start.1 = (bf16[256,2,128]{2,0,1:T(8,128)(2,1)S(1)}, bf16[256,2,128]{2,0,1:T(8,128)(2,1)S(1)}, u32[]{:S(2)}, u32[]{:S(2)}) collective-permute-start(bf16[256,2,128]{2,0,1:T(8,128)(2,1)S(1)} %get-tuple-element.309), channel_id=1, source_target_pairs={{0,4},{4,8},{8,12},{12,16},{16,20},{20,24},{24,28},{1,5},{5,9},{9,... | collective-permute-start | bytes 393224 | tf_op jit(solution)/shard_map/while/body/eval_jaxpr/ppermute | solution.py:16
  85.0 1.4 %fusion.40 = (f32[2,2,256]{2,1,0:T(2,128)S(1)}, bf16[2,2,256,256]{2,3,1,0:T(8,128)(2,1)S(1)}) fusion(bf16[256,2,2,128]{3,0,2,1:T(8,128)(2,1)} %get-tuple-element.323, bf16[256,2,128]{2,0,1:T(8,128)(2,1)S(1)} %collective-permute-done, pred[256,256]{0,1:T(8,128)(4,1)S(1)} %fusion.39), kind=kOutput, calls=%fused_computation.49.clone.1 | convolution fusion | flops 68418560 | bytes 987136 | tf_op jit(solution)/shard_map/while/body/eval_jaxpr/sgrh,kgh->grsk/dot_general | solution.py:41
  88.6 4.3 %collective-permute-start = (bf16[256,2,128]{2,0,1:T(8,128)(2,1)}, bf16[256,2,128]{2,0,1:T(8,128)(2,1)S(1)}, u32[]{:S(2)}, u32[]{:S(2)}) collective-permute-start(bf16[256,2,128]{2,0,1:T(8,128)(2,1)} %get-tuple-element.308), channel_id=1, source_target_pairs={{0,4},{4,8},{8,12},{12,16},{16,20},{20,24},{24,28},{1,5},{5,9},{9,... | collective-permute-start | bytes 393224 | tf_op jit(solution)/shard_map/while/body/eval_jaxpr/ppermute | solution.py:16
  92.9 4.6 %collective-permute-start.1 = (bf16[256,2,128]{2,0,1:T(8,128)(2,1)S(1)}, bf16[256,2,128]{2,0,1:T(8,128)(2,1)S(1)}, u32[]{:S(2)}, u32[]{:S(2)}) collective-permute-start(bf16[256,2,128]{2,0,1:T(8,128)(2,1)S(1)} %get-tuple-element.309), channel_id=1, source_target_pairs={{0,4},{4,8},{8,12},{12,16},{16,20},{20,24},{24,28},{1,5},{5,9},{9,... | collective-permute-start | bytes 393224 | tf_op jit(solution)/shard_map/while/body/eval_jaxpr/ppermute | solution.py:16
  97.7 1.4 %fusion.40 = (f32[2,2,256]{2,1,0:T(2,128)S(1)}, bf16[2,2,256,256]{2,3,1,0:T(8,128)(2,1)S(1)}) fusion(bf16[256,2,2,128]{3,0,2,1:T(8,128)(2,1)} %get-tuple-element.323, bf16[256,2,128]{2,0,1:T(8,128)(2,1)S(1)} %collective-permute-done, pred[256,256]{0,1:T(8,128)(4,1)S(1)} %fusion.39), kind=kOutput, calls=%fused_computation.49.clone.1 | convolution fusion | flops 68418560 | bytes 987136 | tf_op jit(solution)/shard_map/while/body/eval_jaxpr/sgrh,kgh->grsk/dot_general | solution.py:41
  101.2 2.0 %divide_convert_fusion = bf16[2,2,256,128]{3,2,1,0:T(8,128)(2,1)} fusion(f32[2,2,256,128]{3,2,1,0:T(8,128)} %get-tuple-element.189, f32[2,2,256]{2,1,0:T(2,128)S(1)} %get-tuple-element.190), kind=kLoop, calls=%fused_computation.26 | loop fusion | flops 262144 | bytes 790528 | tf_op jit(solution)/shard_map/convert_element_type | solution.py:97
  103.9 15.4 %all-gather.2.cloned.1.call-done = bf16[256,16,128]{2,0,1:T(8,128)(2,1)} async-done(((bf16[256,4,128]{2,0,1:T(8,128)(2,1)}), bf16[256,16,128]{2,0,1:T(8,128)(2,1)}) %all-gather.2.cloned.1.call-update) | async-done | bytes 1048592 | tf_op jit(solution)/shard_map/all_gather | solution.py:100
  119.3 3.1 %multiply_reduce_fusion = (f32[256]{0:T(256)S(1)}, f32[256,768]{1,0:T(8,128)}) fusion(bf16[256,16,128]{2,0,1:T(8,128)(2,1)} %all-gather.2.cloned.1.call-done, bf16[16,128,768]{2,1,0:T(8,128)(2,1)S(1)} %copy-done), kind=kOutput, calls=%fused_computation.25 | convolution fusion | flops 805699328 | bytes 4981760 | tf_op jit(solution)/shard_map/dot_general | solution.py:103
  122.4 5.9 %psum.7 = f32[256]{0:T(256)S(1)} all-reduce(f32[256]{0:T(256)S(1)} %get-tuple-element.233), channel_id=1, replica_groups=mesh['ctx'=8,'tp'=4] {'tp'}, use_global_device_ids=true, to_apply=%region_5.6 | all-reduce | flops 256 | bytes 2048 | tf_op jit(solution)/shard_map/psum | solution.py:106
  128.3 2.1 %add_convert_fusion = bf16[256,768]{1,0:T(8,128)(2,1)} fusion(f32[256,768]{1,0:T(8,128)} %get-tuple-element.234, bf16[256,768]{1,0:T(8,128)(2,1)S(1)} %copy-done.4, f32[768]{0:T(1024)S(1)} %convert_element_type.50, f32[256]{0:T(256)S(1)} %add_rsqrt_fusion), kind=kLoop, calls=%fused_computation.24 | loop fusion | flops 983040 | bytes 1576960 | tf_op jit(solution)/shard_map/convert_element_type | solution.py:109
  (133 shorter events, 30.1 us)
Async XLA Ops:
  6.5 112.8 %copy-start = (bf16[16,128,768]{2,1,0:T(8,128)(2,1)S(1)}, bf16[16,128,768]{2,1,0:T(8,128)(2,1)}, u32[]{:S(2)}) copy-start(bf16[16,128,768]{2,1,0:T(8,128)(2,1)} %param.12) | copy-start | bytes 9437188
  6.5 4.8 %copy-start.3 = (bf16[256,2,128]{2,1,0:T(2,128)(2,1)S(1)}, bf16[256,2,128]{2,1,0:T(2,128)(2,1)}, u32[]{:S(2)}) copy-start(bf16[256,2,128]{2,1,0:T(2,128)(2,1)} %param.10) | copy-start | bytes 393220
  6.5 112.8 %all-gather.2.cloned.1.call-start = ((), (), s32[]{:S(2)}) async-start(), calls=%async_computation | async-start | bytes 1310720 | tf_op jit(solution)/shard_map/all_gather | solution.py:100
  13.1 3.0 %copy-start.6 = (bf16[256,2,128]{2,0,1:T(8,128)(2,1)}, bf16[256,2,128]{2,0,1:T(8,128)(2,1)S(1)}, u32[]{:S(2)}) copy-start(bf16[256,2,128]{2,0,1:T(8,128)(2,1)S(1)} %pad_maximum_fusion.1) | copy-start | bytes 393220
  16.1 8.5 %collective-permute-start = (bf16[256,2,128]{2,0,1:T(8,128)(2,1)}, bf16[256,2,128]{2,0,1:T(8,128)(2,1)S(1)}, u32[]{:S(2)}, u32[]{:S(2)}) collective-permute-start(bf16[256,2,128]{2,0,1:T(8,128)(2,1)} %get-tuple-element.308), channel_id=1, source_target_pairs={{0,4},{4,8},{8,12},{12,16},{16,20},{20,24},{24,28},{1,5},{5,9},{9,... | collective-permute-start | bytes 393224 | tf_op jit(solution)/shard_map/while/body/eval_jaxpr/ppermute | solution.py:16
  21.0 5.9 %collective-permute-start.1 = (bf16[256,2,128]{2,0,1:T(8,128)(2,1)S(1)}, bf16[256,2,128]{2,0,1:T(8,128)(2,1)S(1)}, u32[]{:S(2)}, u32[]{:S(2)}) collective-permute-start(bf16[256,2,128]{2,0,1:T(8,128)(2,1)S(1)} %get-tuple-element.309), channel_id=1, source_target_pairs={{0,4},{4,8},{8,12},{12,16},{16,20},{20,24},{24,28},{1,5},{5,9},{9,... | collective-permute-start | bytes 393224 | tf_op jit(solution)/shard_map/while/body/eval_jaxpr/ppermute | solution.py:16
  24.5 2.5 %copy-start.1 = (f32[2,2,256,128]{3,2,1,0:T(8,128)S(1)}, f32[2,2,256,128]{3,2,1,0:T(8,128)}, u32[]{:S(2)}) copy-start(f32[2,2,256,128]{3,2,1,0:T(8,128)} %get-tuple-element.306) | copy-start | bytes 1572868 | tf_op jit(solution)/shard_map/while
  28.2 8.9 %collective-permute-start = (bf16[256,2,128]{2,0,1:T(8,128)(2,1)}, bf16[256,2,128]{2,0,1:T(8,128)(2,1)S(1)}, u32[]{:S(2)}, u32[]{:S(2)}) collective-permute-start(bf16[256,2,128]{2,0,1:T(8,128)(2,1)} %get-tuple-element.308), channel_id=1, source_target_pairs={{0,4},{4,8},{8,12},{12,16},{16,20},{20,24},{24,28},{1,5},{5,9},{9,... | collective-permute-start | bytes 393224 | tf_op jit(solution)/shard_map/while/body/eval_jaxpr/ppermute | solution.py:16
  32.5 6.8 %collective-permute-start.1 = (bf16[256,2,128]{2,0,1:T(8,128)(2,1)S(1)}, bf16[256,2,128]{2,0,1:T(8,128)(2,1)S(1)}, u32[]{:S(2)}, u32[]{:S(2)}) collective-permute-start(bf16[256,2,128]{2,0,1:T(8,128)(2,1)S(1)} %get-tuple-element.309), channel_id=1, source_target_pairs={{0,4},{4,8},{8,12},{12,16},{16,20},{20,24},{24,28},{1,5},{5,9},{9,... | collective-permute-start | bytes 393224 | tf_op jit(solution)/shard_map/while/body/eval_jaxpr/ppermute | solution.py:16
  36.9 2.5 %copy-start.1 = (f32[2,2,256,128]{3,2,1,0:T(8,128)S(1)}, f32[2,2,256,128]{3,2,1,0:T(8,128)}, u32[]{:S(2)}) copy-start(f32[2,2,256,128]{3,2,1,0:T(8,128)} %get-tuple-element.306) | copy-start | bytes 1572868 | tf_op jit(solution)/shard_map/while
  40.6 8.7 %collective-permute-start = (bf16[256,2,128]{2,0,1:T(8,128)(2,1)}, bf16[256,2,128]{2,0,1:T(8,128)(2,1)S(1)}, u32[]{:S(2)}, u32[]{:S(2)}) collective-permute-start(bf16[256,2,128]{2,0,1:T(8,128)(2,1)} %get-tuple-element.308), channel_id=1, source_target_pairs={{0,4},{4,8},{8,12},{12,16},{16,20},{20,24},{24,28},{1,5},{5,9},{9,... | collective-permute-start | bytes 393224 | tf_op jit(solution)/shard_map/while/body/eval_jaxpr/ppermute | solution.py:16
  45.0 6.6 %collective-permute-start.1 = (bf16[256,2,128]{2,0,1:T(8,128)(2,1)S(1)}, bf16[256,2,128]{2,0,1:T(8,128)(2,1)S(1)}, u32[]{:S(2)}, u32[]{:S(2)}) collective-permute-start(bf16[256,2,128]{2,0,1:T(8,128)(2,1)S(1)} %get-tuple-element.309), channel_id=1, source_target_pairs={{0,4},{4,8},{8,12},{12,16},{16,20},{20,24},{24,28},{1,5},{5,9},{9,... | collective-permute-start | bytes 393224 | tf_op jit(solution)/shard_map/while/body/eval_jaxpr/ppermute | solution.py:16
  49.1 2.5 %copy-start.1 = (f32[2,2,256,128]{3,2,1,0:T(8,128)S(1)}, f32[2,2,256,128]{3,2,1,0:T(8,128)}, u32[]{:S(2)}) copy-start(f32[2,2,256,128]{3,2,1,0:T(8,128)} %get-tuple-element.306) | copy-start | bytes 1572868 | tf_op jit(solution)/shard_map/while
  52.8 8.2 %collective-permute-start = (bf16[256,2,128]{2,0,1:T(8,128)(2,1)}, bf16[256,2,128]{2,0,1:T(8,128)(2,1)S(1)}, u32[]{:S(2)}, u32[]{:S(2)}) collective-permute-start(bf16[256,2,128]{2,0,1:T(8,128)(2,1)} %get-tuple-element.308), channel_id=1, source_target_pairs={{0,4},{4,8},{8,12},{12,16},{16,20},{20,24},{24,28},{1,5},{5,9},{9,... | collective-permute-start | bytes 393224 | tf_op jit(solution)/shard_map/while/body/eval_jaxpr/ppermute | solution.py:16
  57.2 6.2 %collective-permute-start.1 = (bf16[256,2,128]{2,0,1:T(8,128)(2,1)S(1)}, bf16[256,2,128]{2,0,1:T(8,128)(2,1)S(1)}, u32[]{:S(2)}, u32[]{:S(2)}) collective-permute-start(bf16[256,2,128]{2,0,1:T(8,128)(2,1)S(1)} %get-tuple-element.309), channel_id=1, source_target_pairs={{0,4},{4,8},{8,12},{12,16},{16,20},{20,24},{24,28},{1,5},{5,9},{9,... | collective-permute-start | bytes 393224 | tf_op jit(solution)/shard_map/while/body/eval_jaxpr/ppermute | solution.py:16
  60.9 2.5 %copy-start.1 = (f32[2,2,256,128]{3,2,1,0:T(8,128)S(1)}, f32[2,2,256,128]{3,2,1,0:T(8,128)}, u32[]{:S(2)}) copy-start(f32[2,2,256,128]{3,2,1,0:T(8,128)} %get-tuple-element.306) | copy-start | bytes 1572868 | tf_op jit(solution)/shard_map/while
  64.6 8.6 %collective-permute-start = (bf16[256,2,128]{2,0,1:T(8,128)(2,1)}, bf16[256,2,128]{2,0,1:T(8,128)(2,1)S(1)}, u32[]{:S(2)}, u32[]{:S(2)}) collective-permute-start(bf16[256,2,128]{2,0,1:T(8,128)(2,1)} %get-tuple-element.308), channel_id=1, source_target_pairs={{0,4},{4,8},{8,12},{12,16},{16,20},{20,24},{24,28},{1,5},{5,9},{9,... | collective-permute-start | bytes 393224 | tf_op jit(solution)/shard_map/while/body/eval_jaxpr/ppermute | solution.py:16
  69.0 6.6 %collective-permute-start.1 = (bf16[256,2,128]{2,0,1:T(8,128)(2,1)S(1)}, bf16[256,2,128]{2,0,1:T(8,128)(2,1)S(1)}, u32[]{:S(2)}, u32[]{:S(2)}) collective-permute-start(bf16[256,2,128]{2,0,1:T(8,128)(2,1)S(1)} %get-tuple-element.309), channel_id=1, source_target_pairs={{0,4},{4,8},{8,12},{12,16},{16,20},{20,24},{24,28},{1,5},{5,9},{9,... | collective-permute-start | bytes 393224 | tf_op jit(solution)/shard_map/while/body/eval_jaxpr/ppermute | solution.py:16
  73.1 2.5 %copy-start.1 = (f32[2,2,256,128]{3,2,1,0:T(8,128)S(1)}, f32[2,2,256,128]{3,2,1,0:T(8,128)}, u32[]{:S(2)}) copy-start(f32[2,2,256,128]{3,2,1,0:T(8,128)} %get-tuple-element.306) | copy-start | bytes 1572868 | tf_op jit(solution)/shard_map/while
  76.8 8.2 %collective-permute-start = (bf16[256,2,128]{2,0,1:T(8,128)(2,1)}, bf16[256,2,128]{2,0,1:T(8,128)(2,1)S(1)}, u32[]{:S(2)}, u32[]{:S(2)}) collective-permute-start(bf16[256,2,128]{2,0,1:T(8,128)(2,1)} %get-tuple-element.308), channel_id=1, source_target_pairs={{0,4},{4,8},{8,12},{12,16},{16,20},{20,24},{24,28},{1,5},{5,9},{9,... | collective-permute-start | bytes 393224 | tf_op jit(solution)/shard_map/while/body/eval_jaxpr/ppermute | solution.py:16
  81.1 6.2 %collective-permute-start.1 = (bf16[256,2,128]{2,0,1:T(8,128)(2,1)S(1)}, bf16[256,2,128]{2,0,1:T(8,128)(2,1)S(1)}, u32[]{:S(2)}, u32[]{:S(2)}) collective-permute-start(bf16[256,2,128]{2,0,1:T(8,128)(2,1)S(1)} %get-tuple-element.309), channel_id=1, source_target_pairs={{0,4},{4,8},{8,12},{12,16},{16,20},{20,24},{24,28},{1,5},{5,9},{9,... | collective-permute-start | bytes 393224 | tf_op jit(solution)/shard_map/while/body/eval_jaxpr/ppermute | solution.py:16
  88.6 9.1 %collective-permute-start = (bf16[256,2,128]{2,0,1:T(8,128)(2,1)}, bf16[256,2,128]{2,0,1:T(8,128)(2,1)S(1)}, u32[]{:S(2)}, u32[]{:S(2)}) collective-permute-start(bf16[256,2,128]{2,0,1:T(8,128)(2,1)} %get-tuple-element.308), channel_id=1, source_target_pairs={{0,4},{4,8},{8,12},{12,16},{16,20},{20,24},{24,28},{1,5},{5,9},{9,... | collective-permute-start | bytes 393224 | tf_op jit(solution)/shard_map/while/body/eval_jaxpr/ppermute | solution.py:16
  92.9 7.1 %collective-permute-start.1 = (bf16[256,2,128]{2,0,1:T(8,128)(2,1)S(1)}, bf16[256,2,128]{2,0,1:T(8,128)(2,1)S(1)}, u32[]{:S(2)}, u32[]{:S(2)}) collective-permute-start(bf16[256,2,128]{2,0,1:T(8,128)(2,1)S(1)} %get-tuple-element.309), channel_id=1, source_target_pairs={{0,4},{4,8},{8,12},{12,16},{16,20},{20,24},{24,28},{1,5},{5,9},{9,... | collective-permute-start | bytes 393224 | tf_op jit(solution)/shard_map/while/body/eval_jaxpr/ppermute | solution.py:16
  101.2 27.1 %copy-start.4 = (bf16[256,768]{1,0:T(8,128)(2,1)S(1)}, bf16[256,768]{1,0:T(8,128)(2,1)}, u32[]{:S(2)}) copy-start(bf16[256,768]{1,0:T(8,128)(2,1)} %param.11) | copy-start | bytes 1179652
  (11 other events, 14.2 us)
Sparse Core Ops, SparseCore 0:
  103.4 15.8 all-gather.1
where the time goes:
time: 138 us; the launch traced here: 137 us
  starting transfers between devices  58.8 us (43%)
  matrix products  17.8 us (13%)
  waiting for transfers between devices  16.7 us (12%)
  between operations  13.5 us (10%)
  other arithmetic  12.3 us (9%)
  local copies, waits for them, and re-layouts  11.6 us (8%)
  blocking collectives  5.85 us (4%)
    ppermute x14, starting transfers between devices, passed_along(): lax.ppermute(value, axis, [(source, source + steps) for source in range(f...  58.8 us
    all_gather x1, waiting for transfers between devices, local(): piece = lax.all_gather(attended, 'tp', axis=1, tiled=True)  15.4 us
    dot_general x8, matrix products, attend_block(): jnp.einsum('sgrh,kgh->grsk', rotary_queries, key_block, preferred_element...  10.6 us
    while x42, local copies, waits for them, and re-layouts  10.1 us
    psum x1, blocking collectives, local(): square_sums = lax.psum(jnp.sum(projected * projected, axis=1), 'tp')  5.85 us
    dot_general x8, matrix products, attend_block(): jnp.einsum('grsk,kgh->grsh', weights.astype(jnp.bfloat16), value_block, p...  4.09 us
    dot_general x1, matrix products, local(): jnp.dot(piece.reshape(rows, heads_in * head_size), weight_rows, preferred...  3.14 us
  transfers between devices with their start and end apart: 15, of which 8 were waited for; matrix products, arithmetic and copies ran while one was open for 12% of the time, Pallas kernels for 0%

commit v1 on v0

--- a/solution.py
+++ b/solution.py
@@ -103,7 +103,7 @@
     projected = jnp.dot(
         piece.reshape(rows, heads_in * head_size), weight_rows, preferred_element_type=jnp.float32
     )
-    square_sums = lax.psum(jnp.sum(projected * projected, axis=1), "tp")
+    square_sums = jnp.sum(lax.all_gather(jnp.sum(projected * projected, axis=1), "tp"), axis=0)
     normed = projected * lax.rsqrt(square_sums / D + 1e-06)[:, None] * post_gain.astype(jnp.float32)
     mixed = residual.astype(jnp.float32) + normed
     return mixed.astype(jnp.bfloat16)

time: 138 us -> 137 us (level)
    psum x1 -> x0, blocking collectives: 5.85 us -> none  [local(): square_sums = lax.psum(jnp.sum(projected * projected, axis=1), 'tp')]
    all_gather x0 -> x1, blocking collectives: none -> 5.06 us  [local(): lax.all_gather(jnp.sum(projected * projected, axis=1), 'tp')]
where the time goes in v1:
time: 137 us; the launch traced here: 136 us
  starting transfers between devices  58.8 us (43%)
  matrix products  17.8 us (13%)
  waiting for transfers between devices  16.7 us (12%)
  between operations  13.5 us (10%)
  other arithmetic  12.3 us (9%)
  local copies, waits for them, and re-layouts  11.6 us (8%)
  blocking collectives  5.06 us (4%)
    ppermute x14, starting transfers between devices, passed_along(): lax.ppermute(value, axis, [(source, source + steps) for source in range(f...  58.8 us
    all_gather x1, waiting for transfers between devices, local(): piece = lax.all_gather(attended, 'tp', axis=1, tiled=True)  15.4 us
    dot_general x8, matrix products, attend_block(): jnp.einsum('sgrh,kgh->grsk', rotary_queries, key_block, preferred_element...  10.6 us
    while x42, local copies, waits for them, and re-layouts  10.1 us
    all_gather x1, blocking collectives, local(): lax.all_gather(jnp.sum(projected * projected, axis=1), 'tp')  5.06 us
    dot_general x8, matrix products, attend_block(): jnp.einsum('grsk,kgh->grsh', weights.astype(jnp.bfloat16), value_block, p...  4.09 us
    dot_general x1, matrix products, local(): jnp.dot(piece.reshape(rows, heads_in * head_size), weight_rows, preferred...  3.14 us
  transfers between devices with their start and end apart: 15, of which 8 were waited for; matrix products, arithmetic and copies ran while one was open for 12% of the time, Pallas kernels for 0%

profile of v1, /device:TPU:0, one launch (start us, length us, event | category | flops | bytes accessed | tf_op | source)
XLA Modules:
  0.0 136.5 jit_solution(18267356902781982223)
XLA Ops:
  16.1 85.1 %while.21 = (s32[]{:T(128)}, f32[2,2,256,128]{3,2,1,0:T(8,128)}, f32[2,2,256]{2,1,0:T(2,128)S(1)}, bf16[256,2,128]{2,0,1:T(8,128)(2,1)}, bf16[256,2,128]{2,0,1:T...) while((s32[]{:T(128)}, f32[2,2,256,128]{3,2,1,0:T(8,128)}, ...), condition=%wide.region_3.4_spmd, body=%wide.region_1.3_spmd.sunk | while | flops 135988224 | bytes 8540965 | solution.py:93
  16.1 4.9 %collective-permute-start = (bf16[256,2,128]{2,0,1:T(8,128)(2,1)}, bf16[256,2,128]{2,0,1:T(8,128)(2,1)S(1)}, u32[]{:S(2)}, u32[]{:S(2)}) collective-permute-start(bf16[256,2,128]{2,0,1:T(8,128)(2,1)} %get-tuple-element.308), channel_id=1, source_target_pairs={{0,4},{4,8},{8,12},{12,16},{16,20},{20,24},{24,28},{1,5},{5,9},{9,... | collective-permute-start | bytes 393224 | tf_op jit(solution)/shard_map/while/body/eval_jaxpr/ppermute | solution.py:16
  21.0 3.4 %collective-permute-start.1 = (bf16[256,2,128]{2,0,1:T(8,128)(2,1)S(1)}, bf16[256,2,128]{2,0,1:T(8,128)(2,1)S(1)}, u32[]{:S(2)}, u32[]{:S(2)}) collective-permute-start(bf16[256,2,128]{2,0,1:T(8,128)(2,1)S(1)} %get-tuple-element.309), channel_id=1, source_target_pairs={{0,4},{4,8},{8,12},{12,16},{16,20},{20,24},{24,28},{1,5},{5,9},{9,... | collective-permute-start | bytes 393224 | tf_op jit(solution)/shard_map/while/body/eval_jaxpr/ppermute | solution.py:16
  24.7 1.4 %fusion.40 = (f32[2,2,256]{2,1,0:T(2,128)S(1)}, bf16[2,2,256,256]{2,3,1,0:T(8,128)(2,1)S(1)}) fusion(bf16[256,2,2,128]{3,0,2,1:T(8,128)(2,1)} %get-tuple-element.323, bf16[256,2,128]{2,0,1:T(8,128)(2,1)S(1)} %collective-permute-done, pred[256,256]{0,1:T(8,128)(4,1)S(1)} %fusion.39), kind=kOutput, calls=%fused_computation.49.clone.1 | convolution fusion | flops 68418560 | bytes 987136 | tf_op jit(solution)/shard_map/while/body/eval_jaxpr/sgrh,kgh->grsk/dot_general | solution.py:41
  28.2 4.3 %collective-permute-start = (bf16[256,2,128]{2,0,1:T(8,128)(2,1)}, bf16[256,2,128]{2,0,1:T(8,128)(2,1)S(1)}, u32[]{:S(2)}, u32[]{:S(2)}) collective-permute-start(bf16[256,2,128]{2,0,1:T(8,128)(2,1)} %get-tuple-element.308), channel_id=1, source_target_pairs={{0,4},{4,8},{8,12},{12,16},{16,20},{20,24},{24,28},{1,5},{5,9},{9,... | collective-permute-start | bytes 393224 | tf_op jit(solution)/shard_map/while/body/eval_jaxpr/ppermute | solution.py:16
  32.5 4.3 %collective-permute-start.1 = (bf16[256,2,128]{2,0,1:T(8,128)(2,1)S(1)}, bf16[256,2,128]{2,0,1:T(8,128)(2,1)S(1)}, u32[]{:S(2)}, u32[]{:S(2)}) collective-permute-start(bf16[256,2,128]{2,0,1:T(8,128)(2,1)S(1)} %get-tuple-element.309), channel_id=1, source_target_pairs={{0,4},{4,8},{8,12},{12,16},{16,20},{20,24},{24,28},{1,5},{5,9},{9,... | collective-permute-start | bytes 393224 | tf_op jit(solution)/shard_map/while/body/eval_jaxpr/ppermute | solution.py:16
  40.6 4.3 %collective-permute-start = (bf16[256,2,128]{2,0,1:T(8,128)(2,1)}, bf16[256,2,128]{2,0,1:T(8,128)(2,1)S(1)}, u32[]{:S(2)}, u32[]{:S(2)}) collective-permute-start(bf16[256,2,128]{2,0,1:T(8,128)(2,1)} %get-tuple-element.308), channel_id=1, source_target_pairs={{0,4},{4,8},{8,12},{12,16},{16,20},{20,24},{24,28},{1,5},{5,9},{9,... | collective-permute-start | bytes 393224 | tf_op jit(solution)/shard_map/while/body/eval_jaxpr/ppermute | solution.py:16
  45.0 4.1 %collective-permute-start.1 = (bf16[256,2,128]{2,0,1:T(8,128)(2,1)S(1)}, bf16[256,2,128]{2,0,1:T(8,128)(2,1)S(1)}, u32[]{:S(2)}, u32[]{:S(2)}) collective-permute-start(bf16[256,2,128]{2,0,1:T(8,128)(2,1)S(1)} %get-tuple-element.309), channel_id=1, source_target_pairs={{0,4},{4,8},{8,12},{12,16},{16,20},{20,24},{24,28},{1,5},{5,9},{9,... | collective-permute-start | bytes 393224 | tf_op jit(solution)/shard_map/while/body/eval_jaxpr/ppermute | solution.py:16
  52.8 4.4 %collective-permute-start = (bf16[256,2,128]{2,0,1:T(8,128)(2,1)}, bf16[256,2,128]{2,0,1:T(8,128)(2,1)S(1)}, u32[]{:S(2)}, u32[]{:S(2)}) collective-permute-start(bf16[256,2,128]{2,0,1:T(8,128)(2,1)} %get-tuple-element.308), channel_id=1, source_target_pairs={{0,4},{4,8},{8,12},{12,16},{16,20},{20,24},{24,28},{1,5},{5,9},{9,... | collective-permute-start | bytes 393224 | tf_op jit(solution)/shard_map/while/body/eval_jaxpr/ppermute | solution.py:16
  57.2 3.7 %collective-permute-start.1 = (bf16[256,2,128]{2,0,1:T(8,128)(2,1)S(1)}, bf16[256,2,128]{2,0,1:T(8,128)(2,1)S(1)}, u32[]{:S(2)}, u32[]{:S(2)}) collective-permute-start(bf16[256,2,128]{2,0,1:T(8,128)(2,1)S(1)} %get-tuple-element.309), channel_id=1, source_target_pairs={{0,4},{4,8},{8,12},{12,16},{16,20},{20,24},{24,28},{1,5},{5,9},{9,... | collective-permute-start | bytes 393224 | tf_op jit(solution)/shard_map/while/body/eval_jaxpr/ppermute | solution.py:16
  61.1 1.4 %fusion.40 = (f32[2,2,256]{2,1,0:T(2,128)S(1)}, bf16[2,2,256,256]{2,3,1,0:T(8,128)(2,1)S(1)}) fusion(bf16[256,2,2,128]{3,0,2,1:T(8,128)(2,1)} %get-tuple-element.323, bf16[256,2,128]{2,0,1:T(8,128)(2,1)S(1)} %collective-permute-done, pred[256,256]{0,1:T(8,128)(4,1)S(1)} %fusion.39), kind=kOutput, calls=%fused_computation.49.clone.1 | convolution fusion | flops 68418560 | bytes 987136 | tf_op jit(solution)/shard_map/while/body/eval_jaxpr/sgrh,kgh->grsk/dot_general | solution.py:41
  64.6 4.3 %collective-permute-start = (bf16[256,2,128]{2,0,1:T(8,128)(2,1)}, bf16[256,2,128]{2,0,1:T(8,128)(2,1)S(1)}, u32[]{:S(2)}, u32[]{:S(2)}) collective-permute-start(bf16[256,2,128]{2,0,1:T(8,128)(2,1)} %get-tuple-element.308), channel_id=1, source_target_pairs={{0,4},{4,8},{8,12},{12,16},{16,20},{20,24},{24,28},{1,5},{5,9},{9,... | collective-permute-start | bytes 393224 | tf_op jit(solution)/shard_map/while/body/eval_jaxpr/ppermute | solution.py:16
  69.0 4.1 %collective-permute-start.1 = (bf16[256,2,128]{2,0,1:T(8,128)(2,1)S(1)}, bf16[256,2,128]{2,0,1:T(8,128)(2,1)S(1)}, u32[]{:S(2)}, u32[]{:S(2)}) collective-permute-start(bf16[256,2,128]{2,0,1:T(8,128)(2,1)S(1)} %get-tuple-element.309), channel_id=1, source_target_pairs={{0,4},{4,8},{8,12},{12,16},{16,20},{20,24},{24,28},{1,5},{5,9},{9,... | collective-permute-start | bytes 393224 | tf_op jit(solution)/shard_map/while/body/eval_jaxpr/ppermute | solution.py:16
  76.8 4.3 %collective-permute-start = (bf16[256,2,128]{2,0,1:T(8,128)(2,1)}, bf16[256,2,128]{2,0,1:T(8,128)(2,1)S(1)}, u32[]{:S(2)}, u32[]{:S(2)}) collective-permute-start(bf16[256,2,128]{2,0,1:T(8,128)(2,1)} %get-tuple-element.308), channel_id=1, source_target_pairs={{0,4},{4,8},{8,12},{12,16},{16,20},{20,24},{24,28},{1,5},{5,9},{9,... | collective-permute-start | bytes 393224 | tf_op jit(solution)/shard_map/while/body/eval_jaxpr/ppermute | solution.py:16
  81.1 3.7 %collective-permute-start.1 = (bf16[256,2,128]{2,0,1:T(8,128)(2,1)S(1)}, bf16[256,2,128]{2,0,1:T(8,128)(2,1)S(1)}, u32[]{:S(2)}, u32[]{:S(2)}) collective-permute-start(bf16[256,2,128]{2,0,1:T(8,128)(2,1)S(1)} %get-tuple-element.309), channel_id=1, source_target_pairs={{0,4},{4,8},{8,12},{12,16},{16,20},{20,24},{24,28},{1,5},{5,9},{9,... | collective-permute-start | bytes 393224 | tf_op jit(solution)/shard_map/while/body/eval_jaxpr/ppermute | solution.py:16
  85.0 1.4 %fusion.40 = (f32[2,2,256]{2,1,0:T(2,128)S(1)}, bf16[2,2,256,256]{2,3,1,0:T(8,128)(2,1)S(1)}) fusion(bf16[256,2,2,128]{3,0,2,1:T(8,128)(2,1)} %get-tuple-element.323, bf16[256,2,128]{2,0,1:T(8,128)(2,1)S(1)} %collective-permute-done, pred[256,256]{0,1:T(8,128)(4,1)S(1)} %fusion.39), kind=kOutput, calls=%fused_computation.49.clone.1 | convolution fusion | flops 68418560 | bytes 987136 | tf_op jit(solution)/shard_map/while/body/eval_jaxpr/sgrh,kgh->grsk/dot_general | solution.py:41
  88.6 4.3 %collective-permute-start = (bf16[256,2,128]{2,0,1:T(8,128)(2,1)}, bf16[256,2,128]{2,0,1:T(8,128)(2,1)S(1)}, u32[]{:S(2)}, u32[]{:S(2)}) collective-permute-start(bf16[256,2,128]{2,0,1:T(8,128)(2,1)} %get-tuple-element.308), channel_id=1, source_target_pairs={{0,4},{4,8},{8,12},{12,16},{16,20},{20,24},{24,28},{1,5},{5,9},{9,... | collective-permute-start | bytes 393224 | tf_op jit(solution)/shard_map/while/body/eval_jaxpr/ppermute | solution.py:16
  92.9 4.6 %collective-permute-start.1 = (bf16[256,2,128]{2,0,1:T(8,128)(2,1)S(1)}, bf16[256,2,128]{2,0,1:T(8,128)(2,1)S(1)}, u32[]{:S(2)}, u32[]{:S(2)}) collective-permute-start(bf16[256,2,128]{2,0,1:T(8,128)(2,1)S(1)} %get-tuple-element.309), channel_id=1, source_target_pairs={{0,4},{4,8},{8,12},{12,16},{16,20},{20,24},{24,28},{1,5},{5,9},{9,... | collective-permute-start | bytes 393224 | tf_op jit(solution)/shard_map/while/body/eval_jaxpr/ppermute | solution.py:16
  97.7 1.4 %fusion.40 = (f32[2,2,256]{2,1,0:T(2,128)S(1)}, bf16[2,2,256,256]{2,3,1,0:T(8,128)(2,1)S(1)}) fusion(bf16[256,2,2,128]{3,0,2,1:T(8,128)(2,1)} %get-tuple-element.323, bf16[256,2,128]{2,0,1:T(8,128)(2,1)S(1)} %collective-permute-done, pred[256,256]{0,1:T(8,128)(4,1)S(1)} %fusion.39), kind=kOutput, calls=%fused_computation.49.clone.1 | convolution fusion | flops 68418560 | bytes 987136 | tf_op jit(solution)/shard_map/while/body/eval_jaxpr/sgrh,kgh->grsk/dot_general | solution.py:41
  101.2 2.0 %divide_convert_fusion = bf16[2,2,256,128]{3,2,1,0:T(8,128)(2,1)} fusion(f32[2,2,256,128]{3,2,1,0:T(8,128)} %get-tuple-element.189, f32[2,2,256]{2,1,0:T(2,128)S(1)} %get-tuple-element.190), kind=kLoop, calls=%fused_computation.26 | loop fusion | flops 262144 | bytes 790528 | tf_op jit(solution)/shard_map/convert_element_type | solution.py:97
  103.9 15.4 %all-gather.4.cloned.1.call-done = bf16[256,16,128]{2,0,1:T(8,128)(2,1)} async-done(((bf16[256,4,128]{2,0,1:T(8,128)(2,1)}), bf16[256,16,128]{2,0,1:T(8,128)(2,1)}) %all-gather.4.cloned.1.call-update) | async-done | bytes 1048592 | tf_op jit(solution)/shard_map/all_gather | solution.py:100
  119.3 3.1 %multiply_reduce_fusion = (f32[256]{0:T(256)S(1)}, f32[256,768]{1,0:T(8,128)}) fusion(bf16[256,16,128]{2,0,1:T(8,128)(2,1)} %all-gather.4.cloned.1.call-done, bf16[16,128,768]{2,1,0:T(8,128)(2,1)S(1)} %copy-done), kind=kOutput, calls=%fused_computation.25 | convolution fusion | flops 805699328 | bytes 4981760 | tf_op jit(solution)/shard_map/dot_general | solution.py:103
  122.4 5.1 %all-gather.1 = f32[4,1,256]{2,1,0:T(1,128)S(1)} all-gather(f32[1,1,256]{2,1,0:T(1,128)S(1)} %bitcast.54), channel_id=2, replica_groups=mesh['ctx'=8,'tp'=4] {'tp'}, dimensions={0}, use_global_device_ids=true | all-gather | bytes 5120 | tf_op jit(solution)/shard_map/all_gather | solution.py:106
  127.5 2.1 %add_convert_fusion = bf16[256,768]{1,0:T(8,128)(2,1)} fusion(f32[256,768]{1,0:T(8,128)} %get-tuple-element.234, bf16[256,768]{1,0:T(8,128)(2,1)S(1)} %copy-done.4, f32[768]{0:T(1024)S(1)} %convert_element_type.50, f32[256]{0:T(256)S(1)} %add_rsqrt_fusion), kind=kLoop, calls=%fused_computation.24 | loop fusion | flops 983040 | bytes 1576960 | tf_op jit(solution)/shard_map/convert_element_type | solution.py:109
  (134 shorter events, 30.1 us)
Async XLA Ops:
  6.5 112.8 %copy-start = (bf16[16,128,768]{2,1,0:T(8,128)(2,1)S(1)}, bf16[16,128,768]{2,1,0:T(8,128)(2,1)}, u32[]{:S(2)}) copy-start(bf16[16,128,768]{2,1,0:T(8,128)(2,1)} %param.12) | copy-start | bytes 9437188
  6.5 4.8 %copy-start.3 = (bf16[256,2,128]{2,1,0:T(2,128)(2,1)S(1)}, bf16[256,2,128]{2,1,0:T(2,128)(2,1)}, u32[]{:S(2)}) copy-start(bf16[256,2,128]{2,1,0:T(2,128)(2,1)} %param.10) | copy-start | bytes 393220
  6.5 112.8 %all-gather.4.cloned.1.call-start = ((), (), s32[]{:S(2)}) async-start(), calls=%async_computation | async-start | bytes 1310720 | tf_op jit(solution)/shard_map/all_gather | solution.py:100
  13.1 3.0 %copy-start.6 = (bf16[256,2,128]{2,0,1:T(8,128)(2,1)}, bf16[256,2,128]{2,0,1:T(8,128)(2,1)S(1)}, u32[]{:S(2)}) copy-start(bf16[256,2,128]{2,0,1:T(8,128)(2,1)S(1)} %pad_maximum_fusion.1) | copy-start | bytes 393220
  16.1 8.5 %collective-permute-start = (bf16[256,2,128]{2,0,1:T(8,128)(2,1)}, bf16[256,2,128]{2,0,1:T(8,128)(2,1)S(1)}, u32[]{:S(2)}, u32[]{:S(2)}) collective-permute-start(bf16[256,2,128]{2,0,1:T(8,128)(2,1)} %get-tuple-element.308), channel_id=1, source_target_pairs={{0,4},{4,8},{8,12},{12,16},{16,20},{20,24},{24,28},{1,5},{5,9},{9,... | collective-permute-start | bytes 393224 | tf_op jit(solution)/shard_map/while/body/eval_jaxpr/ppermute | solution.py:16
  21.0 5.9 %collective-permute-start.1 = (bf16[256,2,128]{2,0,1:T(8,128)(2,1)S(1)}, bf16[256,2,128]{2,0,1:T(8,128)(2,1)S(1)}, u32[]{:S(2)}, u32[]{:S(2)}) collective-permute-start(bf16[256,2,128]{2,0,1:T(8,128)(2,1)S(1)} %get-tuple-element.309), channel_id=1, source_target_pairs={{0,4},{4,8},{8,12},{12,16},{16,20},{20,24},{24,28},{1,5},{5,9},{9,... | collective-permute-start | bytes 393224 | tf_op jit(solution)/shard_map/while/body/eval_jaxpr/ppermute | solution.py:16
  24.5 2.5 %copy-start.1 = (f32[2,2,256,128]{3,2,1,0:T(8,128)S(1)}, f32[2,2,256,128]{3,2,1,0:T(8,128)}, u32[]{:S(2)}) copy-start(f32[2,2,256,128]{3,2,1,0:T(8,128)} %get-tuple-element.306) | copy-start | bytes 1572868 | tf_op jit(solution)/shard_map/while
  28.2 8.9 %collective-permute-start = (bf16[256,2,128]{2,0,1:T(8,128)(2,1)}, bf16[256,2,128]{2,0,1:T(8,128)(2,1)S(1)}, u32[]{:S(2)}, u32[]{:S(2)}) collective-permute-start(bf16[256,2,128]{2,0,1:T(8,128)(2,1)} %get-tuple-element.308), channel_id=1, source_target_pairs={{0,4},{4,8},{8,12},{12,16},{16,20},{20,24},{24,28},{1,5},{5,9},{9,... | collective-permute-start | bytes 393224 | tf_op jit(solution)/shard_map/while/body/eval_jaxpr/ppermute | solution.py:16
  32.5 6.8 %collective-permute-start.1 = (bf16[256,2,128]{2,0,1:T(8,128)(2,1)S(1)}, bf16[256,2,128]{2,0,1:T(8,128)(2,1)S(1)}, u32[]{:S(2)}, u32[]{:S(2)}) collective-permute-start(bf16[256,2,128]{2,0,1:T(8,128)(2,1)S(1)} %get-tuple-element.309), channel_id=1, source_target_pairs={{0,4},{4,8},{8,12},{12,16},{16,20},{20,24},{24,28},{1,5},{5,9},{9,... | collective-permute-start | bytes 393224 | tf_op jit(solution)/shard_map/while/body/eval_jaxpr/ppermute | solution.py:16
  36.9 2.5 %copy-start.1 = (f32[2,2,256,128]{3,2,1,0:T(8,128)S(1)}, f32[2,2,256,128]{3,2,1,0:T(8,128)}, u32[]{:S(2)}) copy-start(f32[2,2,256,128]{3,2,1,0:T(8,128)} %get-tuple-element.306) | copy-start | bytes 1572868 | tf_op jit(solution)/shard_map/while
  40.6 8.7 %collective-permute-start = (bf16[256,2,128]{2,0,1:T(8,128)(2,1)}, bf16[256,2,128]{2,0,1:T(8,128)(2,1)S(1)}, u32[]{:S(2)}, u32[]{:S(2)}) collective-permute-start(bf16[256,2,128]{2,0,1:T(8,128)(2,1)} %get-tuple-element.308), channel_id=1, source_target_pairs={{0,4},{4,8},{8,12},{12,16},{16,20},{20,24},{24,28},{1,5},{5,9},{9,... | collective-permute-start | bytes 393224 | tf_op jit(solution)/shard_map/while/body/eval_jaxpr/ppermute | solution.py:16
  45.0 6.6 %collective-permute-start.1 = (bf16[256,2,128]{2,0,1:T(8,128)(2,1)S(1)}, bf16[256,2,128]{2,0,1:T(8,128)(2,1)S(1)}, u32[]{:S(2)}, u32[]{:S(2)}) collective-permute-start(bf16[256,2,128]{2,0,1:T(8,128)(2,1)S(1)} %get-tuple-element.309), channel_id=1, source_target_pairs={{0,4},{4,8},{8,12},{12,16},{16,20},{20,24},{24,28},{1,5},{5,9},{9,... | collective-permute-start | bytes 393224 | tf_op jit(solution)/shard_map/while/body/eval_jaxpr/ppermute | solution.py:16
  49.1 2.5 %copy-start.1 = (f32[2,2,256,128]{3,2,1,0:T(8,128)S(1)}, f32[2,2,256,128]{3,2,1,0:T(8,128)}, u32[]{:S(2)}) copy-start(f32[2,2,256,128]{3,2,1,0:T(8,128)} %get-tuple-element.306) | copy-start | bytes 1572868 | tf_op jit(solution)/shard_map/while
  52.8 8.2 %collective-permute-start = (bf16[256,2,128]{2,0,1:T(8,128)(2,1)}, bf16[256,2,128]{2,0,1:T(8,128)(2,1)S(1)}, u32[]{:S(2)}, u32[]{:S(2)}) collective-permute-start(bf16[256,2,128]{2,0,1:T(8,128)(2,1)} %get-tuple-element.308), channel_id=1, source_target_pairs={{0,4},{4,8},{8,12},{12,16},{16,20},{20,24},{24,28},{1,5},{5,9},{9,... | collective-permute-start | bytes 393224 | tf_op jit(solution)/shard_map/while/body/eval_jaxpr/ppermute | solution.py:16
  57.2 6.2 %collective-permute-start.1 = (bf16[256,2,128]{2,0,1:T(8,128)(2,1)S(1)}, bf16[256,2,128]{2,0,1:T(8,128)(2,1)S(1)}, u32[]{:S(2)}, u32[]{:S(2)}) collective-permute-start(bf16[256,2,128]{2,0,1:T(8,128)(2,1)S(1)} %get-tuple-element.309), channel_id=1, source_target_pairs={{0,4},{4,8},{8,12},{12,16},{16,20},{20,24},{24,28},{1,5},{5,9},{9,... | collective-permute-start | bytes 393224 | tf_op jit(solution)/shard_map/while/body/eval_jaxpr/ppermute | solution.py:16
  60.9 2.5 %copy-start.1 = (f32[2,2,256,128]{3,2,1,0:T(8,128)S(1)}, f32[2,2,256,128]{3,2,1,0:T(8,128)}, u32[]{:S(2)}) copy-start(f32[2,2,256,128]{3,2,1,0:T(8,128)} %get-tuple-element.306) | copy-start | bytes 1572868 | tf_op jit(solution)/shard_map/while
  64.6 8.6 %collective-permute-start = (bf16[256,2,128]{2,0,1:T(8,128)(2,1)}, bf16[256,2,128]{2,0,1:T(8,128)(2,1)S(1)}, u32[]{:S(2)}, u32[]{:S(2)}) collective-permute-start(bf16[256,2,128]{2,0,1:T(8,128)(2,1)} %get-tuple-element.308), channel_id=1, source_target_pairs={{0,4},{4,8},{8,12},{12,16},{16,20},{20,24},{24,28},{1,5},{5,9},{9,... | collective-permute-start | bytes 393224 | tf_op jit(solution)/shard_map/while/body/eval_jaxpr/ppermute | solution.py:16
  69.0 6.6 %collective-permute-start.1 = (bf16[256,2,128]{2,0,1:T(8,128)(2,1)S(1)}, bf16[256,2,128]{2,0,1:T(8,128)(2,1)S(1)}, u32[]{:S(2)}, u32[]{:S(2)}) collective-permute-start(bf16[256,2,128]{2,0,1:T(8,128)(2,1)S(1)} %get-tuple-element.309), channel_id=1, source_target_pairs={{0,4},{4,8},{8,12},{12,16},{16,20},{20,24},{24,28},{1,5},{5,9},{9,... | collective-permute-start | bytes 393224 | tf_op jit(solution)/shard_map/while/body/eval_jaxpr/ppermute | solution.py:16
  73.1 2.5 %copy-start.1 = (f32[2,2,256,128]{3,2,1,0:T(8,128)S(1)}, f32[2,2,256,128]{3,2,1,0:T(8,128)}, u32[]{:S(2)}) copy-start(f32[2,2,256,128]{3,2,1,0:T(8,128)} %get-tuple-element.306) | copy-start | bytes 1572868 | tf_op jit(solution)/shard_map/while
  76.8 8.2 %collective-permute-start = (bf16[256,2,128]{2,0,1:T(8,128)(2,1)}, bf16[256,2,128]{2,0,1:T(8,128)(2,1)S(1)}, u32[]{:S(2)}, u32[]{:S(2)}) collective-permute-start(bf16[256,2,128]{2,0,1:T(8,128)(2,1)} %get-tuple-element.308), channel_id=1, source_target_pairs={{0,4},{4,8},{8,12},{12,16},{16,20},{20,24},{24,28},{1,5},{5,9},{9,... | collective-permute-start | bytes 393224 | tf_op jit(solution)/shard_map/while/body/eval_jaxpr/ppermute | solution.py:16
  81.1 6.2 %collective-permute-start.1 = (bf16[256,2,128]{2,0,1:T(8,128)(2,1)S(1)}, bf16[256,2,128]{2,0,1:T(8,128)(2,1)S(1)}, u32[]{:S(2)}, u32[]{:S(2)}) collective-permute-start(bf16[256,2,128]{2,0,1:T(8,128)(2,1)S(1)} %get-tuple-element.309), channel_id=1, source_target_pairs={{0,4},{4,8},{8,12},{12,16},{16,20},{20,24},{24,28},{1,5},{5,9},{9,... | collective-permute-start | bytes 393224 | tf_op jit(solution)/shard_map/while/body/eval_jaxpr/ppermute | solution.py:16
  88.6 9.1 %collective-permute-start = (bf16[256,2,128]{2,0,1:T(8,128)(2,1)}, bf16[256,2,128]{2,0,1:T(8,128)(2,1)S(1)}, u32[]{:S(2)}, u32[]{:S(2)}) collective-permute-start(bf16[256,2,128]{2,0,1:T(8,128)(2,1)} %get-tuple-element.308), channel_id=1, source_target_pairs={{0,4},{4,8},{8,12},{12,16},{16,20},{20,24},{24,28},{1,5},{5,9},{9,... | collective-permute-start | bytes 393224 | tf_op jit(solution)/shard_map/while/body/eval_jaxpr/ppermute | solution.py:16
  92.9 7.1 %collective-permute-start.1 = (bf16[256,2,128]{2,0,1:T(8,128)(2,1)S(1)}, bf16[256,2,128]{2,0,1:T(8,128)(2,1)S(1)}, u32[]{:S(2)}, u32[]{:S(2)}) collective-permute-start(bf16[256,2,128]{2,0,1:T(8,128)(2,1)S(1)} %get-tuple-element.309), channel_id=1, source_target_pairs={{0,4},{4,8},{8,12},{12,16},{16,20},{20,24},{24,28},{1,5},{5,9},{9,... | collective-permute-start | bytes 393224 | tf_op jit(solution)/shard_map/while/body/eval_jaxpr/ppermute | solution.py:16
  101.2 26.3 %copy-start.4 = (bf16[256,768]{1,0:T(8,128)(2,1)S(1)}, bf16[256,768]{1,0:T(8,128)(2,1)}, u32[]{:S(2)}) copy-start(bf16[256,768]{1,0:T(8,128)(2,1)} %param.11) | copy-start | bytes 1179652
  (11 other events, 14.2 us)
Sparse Core Ops, SparseCore 0:
  103.4 15.8 all-gather.3
